TPU v7x, 128 devices: a whole 4x4x4 slice. The times are simulated.
128 devices in a mesh: leaf: 128 (over y, x, z, core).
Axes of the slice: x: 4, y: 4, z: 4, core: 2. Of those that a mesh axis runs over, the one named last changes fastest.
Arguments:
- values: bfloat16 [32768, 8, 128], P('leaf'), may hold values from -6 to 6
- points: bfloat16 [32768, 2, 128], P('leaf'), may hold values from 0 to 6
- basis: bfloat16 [32768, 64, 128], P('leaf'), may hold values from -0.5 to 0.5
- leaf_up: bfloat16 [32768, 4096], P('leaf'), may hold values from -0.5 to 0.5
- mid_up: bfloat16 [8192, 4096], P('leaf'), may hold values from -0.5 to 0.5
- box_up: bfloat16 [2048, 4096], P('leaf'), may hold values from -0.5 to 0.5
- leaf_skel: bfloat16 [32768, 128], P('leaf'), may hold values from 0 to 6
- mid_skel: bfloat16 [8192, 128], P('leaf'), may hold values from 0 to 6
- box_skel: bfloat16 [2048, 128], P('leaf'), may hold values from 0 to 6
- top_skel: bfloat16 [512, 128], replicated, may hold values from 0 to 6
- near_src: int32 [32768, 9], P('leaf'), may hold values from 0 to 32767, as said below
- near_count: int32 [32768], P('leaf'), may hold values from 1 to 9
- leaf_src: int32 [32768, 27], P('leaf'), may hold values from 0 to 32767, as said below
- leaf_count: int32 [32768], P('leaf'), may hold values from 1 to 27
- mid_src: int32 [8192, 27], P('leaf'), may hold values from 0 to 8191, as said below
- mid_count: int32 [8192], P('leaf'), may hold values from 1 to 27
- box_src: int32 [2048, 27], P('leaf'), may hold values from 0 to 2047, as said below
- box_count: int32 [2048], P('leaf'), may hold values from 1 to 27
- box_parent: int32 [2048], replicated, may hold values from 0 to 511, as said below
- top_src: int32 [512, 27], P('leaf'), may hold values from 0 to 511
- top_count: int32 [512], P('leaf'), may hold values from 1 to 27
Outputs:
- potential: float32 [32768, 8, 128], P('leaf')
Inputs may be any that keep to these rules, and one draw needn't show every extreme that they name: `near_src`: every entry of a leaf's list lies on the device of that leaf or on one of the two beside it along leaf; slots past the count hold valid indices too. `leaf_src`: every entry lies on the device of its node or on one of the two beside it along leaf. `mid_src`: every entry lies on the device of its node or on one of the two beside it along leaf. `box_src`: every entry lies on the device of its node or on one of the two beside it along leaf. `box_parent`: every top node is the parent of exactly four level-two nodes, and these are the boxes 4k .. 4k + 3 for some k, all held on one device.
All inputs are finite; a program needn't handle non-finite values.
Results may differ from a plain program's by a relative error of at most 0.0095.
Values may be sent and summed in bfloat16 or wider, within the bound.
No kernel may reach another device: no remote copies, remote signals or barrier semaphores. Data moves between devices by JAX's collectives and lax.ppermute only.
A program may use at most 64 MiB of HBM per device.

v0:
```python
import functools

import jax
import jax.numpy as jnp
from jax import lax
from jax.experimental import pallas as pl
from jax.experimental.pallas import tpu as pltpu
from jax.sharding import PartitionSpec as P


def padded(shard, sides, width):
    for axis, dim in sides:
        size, length = (lax.axis_size(axis), shard.shape[dim])
        up = [(i, (i + 1) % size) for i in range(size - 1)]
        down = [(j, i) for i, j in up]
        last = lax.slice_in_dim(shard, length - width, length, axis=dim)
        leading = lax.slice_in_dim(shard, 0, width, axis=dim)
        before = lax.ppermute(last, axis, up)
        after = lax.ppermute(leading, axis, down)
        shard = jnp.concatenate([before, shard, after], axis=dim)
    return shard


def gather_rows(block, axis):
    size = lax.axis_size(axis)
    rows = block.shape[0]
    full = jnp.zeros((rows * size,) + block.shape[1:], block.dtype)
    full = lax.dynamic_update_slice_in_dim(full, block, lax.axis_index(axis) * rows, axis=0)
    return lax.psum(full, axis)


def lift_up(coeffs, transfer, rank_width):
    nodes = coeffs.shape[0]
    matrices = transfer.reshape(nodes, rank_width, rank_width)
    return jnp.einsum("nsq,nqr->nsr", coeffs, matrices, preferred_element_type=jnp.float32)


NEG_LOG2E = -1.4426950408889634


def coupling(d2):
    return jnp.exp2((d2 * lax.rsqrt(d2)) * NEG_LOG2E).astype(jnp.bfloat16)


def nt_dot(a, b):
    return lax.dot_general(a, b, (((1,), (1,)), ((), ())), preferred_element_type=jnp.float32)


NEAR_UNROLL = 9
FAR_UNROLL = 7


def near_kernel(base_ref, src_ref, cnt_ref, vals_ref, rows_ref, tgt_ref, out_ref, *, slots):
    targets = out_ref.shape[0]
    zeros_v = jnp.zeros(vals_ref.shape[1:], vals_ref.dtype)

    def per_target(t, carry):
        frame = jnp.transpose(tgt_ref[t].astype(jnp.float32)).astype(jnp.bfloat16)
        count = cnt_ref[t]

        def step(i, acc):
            picks = [NEAR_UNROLL * i + u for u in range(NEAR_UNROLL)]
            held = [src_ref[t * slots + jnp.minimum(k, slots - 1)] for k in picks]
            d2s = [jnp.dot(frame, rows_ref[s], preferred_element_type=jnp.float32) for s in held]
            tiles = [coupling(d2) for d2 in d2s]
            for k, s, tile in zip(picks, held, tiles):
                v = jnp.where(k < count, vals_ref[s], zeros_v)
                acc = acc + nt_dot(v, tile)
            return acc

        steps = (count + NEAR_UNROLL - 1) // NEAR_UNROLL
        acc = lax.fori_loop(0, steps, step, jnp.zeros(out_ref.shape[1:], jnp.float32))
        out_ref[t] = 0.25 * acc
        return carry

    lax.fori_loop(0, targets, per_target, 0)


def far_kernel(base_ref, src_ref, cnt_ref, cd_ref, rows_ref, tgt_ref, out_ref, *, slots):
    targets, samples, rank = out_ref.shape
    width = cd_ref.shape[2]
    first_half = lax.broadcasted_iota(jnp.int32, (cd_ref.shape[1], width), 1) < rank
    zeros_c = jnp.zeros((cd_ref.shape[1], width), cd_ref.dtype)
    base = base_ref[0]

    def per_target(t, carry):
        frame = jnp.transpose(tgt_ref[base + t].astype(jnp.float32))[:rank].astype(jnp.bfloat16)
        count = cnt_ref[t]

        def source(k):
            return src_ref[t * slots + jnp.minimum(k, slots - 1)]

        def step(i, acc):
            firsts = [2 * (FAR_UNROLL * i + u) for u in range(FAR_UNROLL)]
            held = [(source(a), source(a + 1)) for a in firsts]
            d2s = [
                jnp.dot(
                    frame,
                    jnp.where(first_half, rows_ref[sa], rows_ref[sb]),
                    preferred_element_type=jnp.float32,
                )
                for sa, sb in held
            ]
            tiles = [coupling(d2) for d2 in d2s]
            for a, (sa, sb), tile in zip(firsts, held, tiles):
                ca = jnp.where(a < count, cd_ref[sa], zeros_c)
                cb = jnp.where(a + 1 < count, cd_ref[sb], zeros_c)
                acc = acc + nt_dot(jnp.where(first_half, ca, cb), tile)
            return acc

        steps = (count + 2 * FAR_UNROLL - 1) // (2 * FAR_UNROLL)
        acc = lax.fori_loop(0, steps, step, jnp.zeros((samples, rank), jnp.float32))
        out_ref[t] = 0.25 * acc
        return carry

    lax.fori_loop(0, targets, per_target, 0)


SMEM = pl.BlockSpec(memory_space=pltpu.SMEM)
VMEM = pl.BlockSpec(memory_space=pltpu.VMEM)


def bf16_split(x):
    hi = lax.reduce_precision(x, exponent_bits=8, mantissa_bits=7)
    rest = x - hi
    mid = lax.reduce_precision(rest, exponent_bits=8, mantissa_bits=7)
    return [hi, mid, rest - mid]


def source_rows(frames):
    x, y = frames[:, 0], frames[:, 1]
    one = jnp.ones_like(x)
    parts = [-2.0 * x, -2.0 * y, one, one, one] + bf16_split(x * x + y * y)
    return jnp.stack(parts, axis=1).astype(jnp.bfloat16)


def target_rows(frames):
    x, y = frames[:, 0], frames[:, 1]
    one = jnp.ones_like(x)
    parts = [x, y] + bf16_split(x * x + y * y + 0.0025) + [one, one, one]
    return jnp.stack(parts, axis=1).astype(jnp.bfloat16)


def near_sum(base, src, counts, vals, rows, tgt):
    targets, slots = src.shape
    samples, width = vals.shape[1], vals.shape[2]
    tile = width * width
    pairs = targets * slots
    return pl.pallas_call(
        functools.partial(near_kernel, slots=slots),
        out_shape=jax.ShapeDtypeStruct((targets, samples, width), jnp.float32),
        in_specs=[SMEM, SMEM, SMEM, VMEM, VMEM, VMEM],
        out_specs=VMEM,
        compiler_params=pltpu.CompilerParams(vmem_limit_bytes=48 * 1024 * 1024),
        cost_estimate=pl.CostEstimate(
            flops=pairs * (2 * (samples + 8) * tile + 3 * tile),
            transcendentals=pairs * 2 * tile,
            bytes_accessed=vals.size * 2 + rows.size * 2 + targets * samples * width * 4,
        ),
    )(base, src.reshape(-1), counts, vals, rows, tgt)


def far_sum(base, src, counts, cd, rows, tgt, rank):
    targets, slots = src.shape
    samples, width = cd.shape[1], cd.shape[2]
    tile = rank * width
    pairs = targets * (slots + 1) // 2
    return pl.pallas_call(
        functools.partial(far_kernel, slots=slots),
        out_shape=jax.ShapeDtypeStruct((targets, samples, rank), jnp.float32),
        in_specs=[SMEM, SMEM, SMEM, VMEM, VMEM, VMEM],
        out_specs=VMEM,
        compiler_params=pltpu.CompilerParams(vmem_limit_bytes=48 * 1024 * 1024),
        cost_estimate=pl.CostEstimate(
            flops=pairs * (2 * (samples + 8) * tile + 3 * tile),
            transcendentals=pairs * 2 * tile,
            bytes_accessed=cd.size * 2 + rows.size * 4 + targets * samples * rank * 4,
        ),
    )(base, src.reshape(-1), counts, cd, rows, tgt)


def far_tables(coef, skel, rank, own=None):
    cd = jnp.concatenate([coef, coef], axis=2)
    frames = skel.astype(jnp.float32).reshape(skel.shape[0], 2, rank)
    rows = source_rows(frames)
    if own is None:
        tgt = target_rows(frames)
    else:
        tgt = target_rows(own.astype(jnp.float32).reshape(own.shape[0], 2, rank))
    return cd, jnp.concatenate([rows, rows], axis=2), jnp.concatenate([tgt, tgt], axis=2)


def body(
    values,
    points,
    basis,
    leaf_up,
    mid_up,
    box_up,
    leaf_skel,
    mid_skel,
    box_skel,
    top_skel,
    near_src,
    near_count,
    leaf_src,
    leaf_count,
    mid_src,
    mid_count,
    box_src,
    box_count,
    box_parent,
    top_src,
    top_count,
):
    leaves = values.shape[0]
    samples = values.shape[1]
    rank_width = basis.shape[1]
    middle = leaves // 4
    box_nodes = leaves // 16
    top_nodes = top_count.shape[0]
    top_all = top_skel.shape[0]
    device = lax.axis_index("leaf")

    near_vals = padded(values, (("leaf", 0),), leaves)
    near_pts = padded(points, (("leaf", 0),), leaves).astype(jnp.float32)
    near_rows = near_src - (device - 1) * leaves
    near_field = near_sum(
        jnp.full((1,), leaves, jnp.int32),
        near_rows,
        near_count,
        near_vals,
        source_rows(near_pts),
        target_rows(points.astype(jnp.float32)),
    )

    leaf_coef = jnp.einsum(
        "tsp,trp->tsr", values, basis, preferred_element_type=jnp.float32
    ).astype(jnp.bfloat16)
    mid_coef = (
        lift_up(leaf_coef, leaf_up, rank_width)
        .reshape(middle, 4, samples, rank_width)
        .sum(axis=1)
        .astype(jnp.bfloat16)
    )
    box_coef = (
        lift_up(mid_coef, mid_up, rank_width)
        .reshape(box_nodes, 4, samples, rank_width)
        .sum(axis=1)
        .astype(jnp.bfloat16)
    )
    box_term = lift_up(box_coef, box_up, rank_width).astype(jnp.bfloat16)
    group_term = (
        box_term.astype(jnp.float32)
        .reshape(box_nodes // 4, 4, samples * rank_width)
        .sum(axis=1)
        .astype(jnp.bfloat16)
    )
    all_groups = gather_rows(group_term, "leaf")
    group_parent = box_parent.reshape(-1, 4)[:, 0]
    select = (
        group_parent[None, :] == jnp.arange(top_all, dtype=jnp.int32)[:, None]
    ).astype(jnp.bfloat16)
    top_coef = jnp.dot(select, all_groups, preferred_element_type=jnp.float32).astype(
        jnp.bfloat16
    )

    def pack(coef, skel):
        return jnp.concatenate([coef.reshape(coef.shape[0], -1), skel], axis=1)

    all_nodes = jnp.concatenate(
        [pack(leaf_coef, leaf_skel), pack(mid_coef, mid_skel), pack(box_coef, box_skel)], axis=0
    )
    per_device = leaves + middle + box_nodes
    node_table = padded(all_nodes, (("leaf", 0),), per_device).reshape(3, per_device, -1)
    coef_width = samples * rank_width

    def level(start, nodes, skel, src, counts):
        rows = node_table[:, start : start + nodes].reshape(3 * nodes, -1)
        coef = rows[:, :coef_width].reshape(3 * nodes, samples, rank_width)
        cd, rows_s, rows_t = far_tables(coef, rows[:, coef_width:], rank_width, skel)
        local = src - (device - 1) * nodes
        return far_sum(jnp.zeros((1,), jnp.int32), local, counts, cd, rows_s, rows_t, rank_width)

    leaf_far = level(0, leaves, leaf_skel, leaf_src, leaf_count)
    mid_far = level(leaves, middle, mid_skel, mid_src, mid_count)
    box_far = level(leaves + middle, box_nodes, box_skel, box_src, box_count)

    top_cd, top_rows, top_tgt = far_tables(
        top_coef.reshape(top_all, samples, rank_width), top_skel, rank_width
    )
    own_field = far_sum(
        (device * top_nodes).astype(jnp.int32).reshape(1),
        top_src,
        top_count,
        top_cd,
        top_rows,
        top_tgt,
        rank_width,
    ).astype(jnp.bfloat16)
    top_field = gather_rows(own_field.reshape(top_nodes, samples * rank_width), "leaf")
    own_parent = lax.dynamic_slice_in_dim(box_parent, device * box_nodes, box_nodes)
    parent_field = top_field[own_parent].reshape(box_nodes, samples, rank_width)
    box_field = (
        box_far
        + jnp.einsum(
            "bsr,bqr->bsq",
            parent_field,
            box_up.reshape(box_nodes, rank_width, rank_width),
            preferred_element_type=jnp.float32,
        )
    ).astype(jnp.bfloat16)
    mid_down = jnp.einsum(
        "bsr,bjqr->bjsq",
        box_field,
        mid_up.reshape(box_nodes, 4, rank_width, rank_width),
        preferred_element_type=jnp.float32,
    )
    mid_field = (mid_far + mid_down.reshape(middle, samples, rank_width)).astype(jnp.bfloat16)
    leaf_down = jnp.einsum(
        "bsr,bjqr->bjsq",
        mid_field,
        leaf_up.reshape(middle, 4, rank_width, rank_width),
        preferred_element_type=jnp.float32,
    )
    leaf_field = (leaf_far + leaf_down.reshape(leaves, samples, rank_width)).astype(jnp.bfloat16)
    return near_field + jnp.einsum(
        "tsr,trp->tsp", leaf_field, basis, preferred_element_type=jnp.float32
    )


def solution(mesh):
    return jax.shard_map(
        body,
        mesh=mesh,
        in_specs=(
            P("leaf", None, None),
            P("leaf", None, None),
            P("leaf", None, None),
            P("leaf", None),
            P("leaf", None),
            P("leaf", None),
            P("leaf", None),
            P("leaf", None),
            P("leaf", None),
            P(),
            P("leaf", None),
            P("leaf"),
            P("leaf", None),
            P("leaf"),
            P("leaf", None),
            P("leaf"),
            P("leaf", None),
            P("leaf"),
            P(),
            P("leaf", None),
            P("leaf"),
        ),
        out_specs=P("leaf", None, None),
        check_vma=False,
    )
```

profile of v0, /device:TPU:22, one launch (start us, length us, event | category | flops | bytes accessed | tf_op | source)
XLA Modules:
  0.0 643.6 jit_solution(16150216482291738541)
XLA Ops:
  6.5 3.3 copy.121
  9.8 6.7 %copy.122 = bf16[256,64,64]{2,1,0:T(8,128)(2,1)} copy(bf16[256,64,64]{0,2,1:T(8,128)(2,1)S(1)} %bitcast.61) | data formatting | bytes 4194304 | tf_op jit(solution)/shard_map/reshape | solution.py:34
  16.5 4.6 convolution_convert_fusion.1
  21.4 3.4 bitcast_reduce_fusion
  30.0 5.8 collective-permute-start.5
  37.7 5.8 collective-permute-start.3
  74.6 5.5 reshape.178
  83.1 6.3 stack.125
  94.6 15.6 %collective-permute-start.1 = (bf16[256,8,128]{2,1,0:T(8,128)(2,1)}, bf16[256,8,128]{2,1,0:T(8,128)(2,1)}, u32[]{:S(2)}, u32[]{:S(2)}) collective-permute-start(bf16[256,8,128]{2,1,0:T(8,128)(2,1)} %param.21), channel_id=1, source_target_pairs={{1,0},{2,1},{3,2},{4,3},{5,4},{6,5},{7,6},{8,7},{9,8},{10,9},{11,1... | collective-permute-start | bytes 1572872 | tf_op jit(solution)/shard_map/ppermute | solution.py:19
  117.6 7.6 %stack.52.rows_ref = bf16[768,8,128]{2,1,0:T(8,128)(2,1)S(1)} concatenate(bf16[768,1,128]{2,1,0:T(2,128)(2,1)} %get-tuple-element.25, bf16[768,1,128]{2,1,0:T(2,128)(2,1)} %get-tuple-element.26, bf16[768,1,128]{2,1,0:T(2,128)(2,1)} %stack_broadcast_in_dim.24, bf16[768,2,128]{2,1,0:T(2,128)(2,1)} %stack.51, bf16[768,1,128]{2,1,0:T(2,128)(2,1)} %get-tuple-element.36, ...), dimensions={1} | concatenate | bytes 3145728 | tf_op jit(solution)/shard_map/stack | solution.py:134
  125.2 72.1 %all-reduce.3.cloned.1.call-done = bf16[512,512]{1,0:T(8,128)(2,1)} async-done(((bf16[512,512]{1,0:T(8,128)(2,1)}), bf16[512,512]{1,0:T(8,128)(2,1)}) %all-reduce.3.cloned.1.call-update) | async-done | bytes 524304 | tf_op jit(solution)/shard_map/psum | solution.py:29
  202.5 3.4 pad_maximum_fusion.3
  205.9 3.0 shard_map.203
  209.9 3.6 concatenate.64
  232.1 3.4 fusion.6
  238.1 2.9 copy.129
  245.7 10.3 %shard_map.202 = f32[16,8,64]{2,1,0:T(8,128)S(1)} custom-call(s32[1]{0:T(128)} %constant.23.clone.1.base_ref, s32[432]{0:T(512)S(1)} %reshape.158.src_ref, s32[16]{0:T(128)S(1)} %copy-done.8, bf16[48,8,128]{2,1,0:T(8,128)(2,1)S(1)} %get-tuple-element.66.cd_ref, bf16[48,8,128]{2,1,0:T(8,128)(2,1)S(1)} %get-tuple-element.67.rows_ref, ...), custom_call_target="tpu_custom_call" | custom-call | flops 64225280 | bytes 327680 | tf_op jit(solution)/shard_map/pallas_call | solution.py:168
  256.0 41.2 %shard_map.201 = f32[64,8,64]{2,1,0:T(8,128)S(1)} custom-call(s32[1]{0:T(128)} %constant.23.clone.1.base_ref, s32[1728]{0:T(1024)S(1)} %copy-done.4, s32[64]{0:T(128)S(1)} %copy-done.9, bf16[192,8,128]{2,1,0:T(8,128)(2,1)S(1)} %get-tuple-element.64.cd_ref, bf16[192,8,128]{2,1,0:T(8,128)(2,1)S(1)} %get-tuple-element.65.rows_ref, ...), custom_call_target="tpu_custom_call" | custom-call | flops 256901120 | bytes 1310720 | tf_op jit(solution)/shard_map/pallas_call | solution.py:168
  299.1 8.5 %stack.56 = bf16[768,8,64]{2,1,0:T(8,128)(2,1)} concatenate(bf16[768,1,64]{2,1,0:T(2,128)(2,1)S(1)} %copy-done.19, bf16[768,1,64]{2,1,0:T(2,128)(2,1)} %get-tuple-element.32, bf16[768,1,64]{2,1,0:T(2,128)(2,1)} %stack_broadcast_in_dim.26, bf16[768,2,64]{2,1,0:T(2,128)(2,1)} %stack.55, bf16[768,1,64]{2,1,0:T(2,128)(2,1)} %get-tuple-element.30, ...), dimensions={1} | concatenate | bytes 1572864 | tf_op jit(solution)/shard_map/stack | solution.py:134
  307.7 4.7 pad_maximum_fusion.1
  312.4 157.0 %shard_map.200 = f32[256,8,64]{2,1,0:T(8,128)S(1)} custom-call(s32[1]{0:T(128)} %constant.23.clone.1.base_ref, s32[6912]{0:T(1024)S(1)} %copy-done.3, s32[256]{0:T(256)S(1)} %copy-done.6, bf16[768,8,128]{2,1,0:T(8,128)(2,1)S(1)} %get-tuple-element.62.cd_ref, bf16[768,8,128]{2,1,0:T(8,128)(2,1)S(1)} %get-tuple-element.63.rows_ref, ...), custom_call_target="tpu_custom_call" | custom-call | flops 1027604480 | bytes 5242880 | tf_op jit(solution)/shard_map/pallas_call | solution.py:168
  471.2 3.1 fusion.3
  475.3 5.7 fusion.14
  483.9 151.6 %shard_map.199 = f32[256,8,128]{2,1,0:T(8,128)S(1)} custom-call(s32[1]{0:T(128)} %constant.16.clone.1.base_ref, s32[2304]{0:T(1024)S(1)} %reshape.137.src_ref, s32[256]{0:T(256)S(1)} %copy-done.7, bf16[768,8,128]{2,1,0:T(8,128)(2,1)S(1)} %pad_maximum_fusion.vals_ref, bf16[768,8,128]{2,1,0:T(8,128)(2,1)S(1)} %stack.52.rows_ref, ...), custom_call_target="tpu_custom_call" | custom-call | flops 1321205760 | bytes 4194304 | tf_op jit(solution)/shard_map/pallas_call | solution.py:149
  (238 shorter events, 94.2 us)
Async XLA Ops:
  6.5 190.8 %all-reduce.3.cloned.1.call-start = ((), (), s32[]{:S(2)}) async-start(), calls=%async_computation | async-start | bytes 1048576 | tf_op jit(solution)/shard_map/psum | solution.py:29
  24.9 20.5 %copy-start.31 = (bf16[16,4096]{1,0:T(8,128)(2,1)S(1)}, bf16[16,4096]{1,0:T(8,128)(2,1)}, u32[]{:S(2)}) copy-start(bf16[16,4096]{1,0:T(8,128)(2,1)} %param.26) | copy-start | bytes 393220
  27.1 23.6 %copy-start.22 = (bf16[256,128]{0,1:T(8,128)(2,1)}, bf16[256,128]{0,1:T(8,128)(2,1)S(1)}, u32[]{:S(2)}) copy-start(bf16[256,128]{0,1:T(8,128)(2,1)S(1)} %copy.120) | copy-start | bytes 196612
  27.2 23.8 %copy-start.32 = (bf16[512,128]{1,0:T(8,128)(2,1)S(1)}, bf16[512,128]{1,0:T(8,128)(2,1)}, u32[]{:S(2)}) copy-start(bf16[512,128]{1,0:T(8,128)(2,1)} %param.30) | copy-start | bytes 393220
  28.1 181.8 %collective-permute-start.4 = (bf16[336,640]{0,1:T(8,128)(2,1)}, bf16[336,640]{0,1:T(8,128)(2,1)}, u32[]{:S(2)}, u32[]{:S(2)}) collective-permute-start(bf16[336,640]{0,1:T(8,128)(2,1)} %pad_maximum_fusion.7), channel_id=1, source_target_pairs={{0,1},{1,2},{2,3},{3,4},{4,5},{5,6},{6,7},{7,8},{8,9},{9,10},{10,1... | collective-permute-start | bytes 1290248 | tf_op jit(solution)/shard_map/ppermute | solution.py:18
  30.0 179.9 %collective-permute-start.5 = (bf16[336,640]{0,1:T(8,128)(2,1)}, bf16[336,640]{0,1:T(8,128)(2,1)}, u32[]{:S(2)}, u32[]{:S(2)}) collective-permute-start(bf16[336,640]{0,1:T(8,128)(2,1)} %pad_maximum_fusion.7), channel_id=1, source_target_pairs={{1,0},{2,1},{3,2},{4,3},{5,4},{6,5},{7,6},{8,7},{9,8},{10,9},{11,1... | collective-permute-start | bytes 1290248 | tf_op jit(solution)/shard_map/ppermute | solution.py:19
  35.8 58.9 %collective-permute-start.2 = (bf16[256,2,128]{2,1,0:T(2,128)(2,1)}, bf16[256,2,128]{2,1,0:T(2,128)(2,1)}, u32[]{:S(2)}, u32[]{:S(2)}) collective-permute-start(bf16[256,2,128]{2,1,0:T(2,128)(2,1)} %param.22), channel_id=1, source_target_pairs={{0,1},{1,2},{2,3},{3,4},{4,5},{5,6},{6,7},{7,8},{8,9},{9,10},{10,1... | collective-permute-start | bytes 393224 | tf_op jit(solution)/shard_map/ppermute | solution.py:18
  37.7 72.5 %collective-permute-start.3 = (bf16[256,2,128]{2,1,0:T(2,128)(2,1)}, bf16[256,2,128]{2,1,0:T(2,128)(2,1)}, u32[]{:S(2)}, u32[]{:S(2)}) collective-permute-start(bf16[256,2,128]{2,1,0:T(2,128)(2,1)} %param.22), channel_id=1, source_target_pairs={{1,0},{2,1},{3,2},{4,3},{5,4},{6,5},{7,6},{8,7},{9,8},{10,9},{11,1... | collective-permute-start | bytes 393224 | tf_op jit(solution)/shard_map/ppermute | solution.py:19
  43.5 438.9 %collective-permute-start = (bf16[256,8,128]{2,1,0:T(8,128)(2,1)}, bf16[256,8,128]{2,1,0:T(8,128)(2,1)}, u32[]{:S(2)}, u32[]{:S(2)}) collective-permute-start(bf16[256,8,128]{2,1,0:T(8,128)(2,1)} %param.21), channel_id=1, source_target_pairs={{0,1},{1,2},{2,3},{3,4},{4,5},{5,6},{6,7},{7,8},{8,9},{9,10},{10,1... | collective-permute-start | bytes 1572872 | tf_op jit(solution)/shard_map/ppermute | solution.py:18
  46.9 422.5 %all-reduce.5.cloned.1.call-start = ((), (), s32[]{:S(2)}) async-start(), calls=%async_computation.1 | async-start | bytes 1048576 | tf_op jit(solution)/shard_map/psum | solution.py:29
  60.9 9.6 %copy-start.41 = (s32[256,9]{0,1:T(8,128)S(1)}, s32[256,9]{0,1:T(8,128)}, u32[]{:S(2)}) copy-start(s32[256,9]{0,1:T(8,128)} %param.31) | copy-start | bytes 27652
  60.9 10.3 %copy-start.42 = (s32[64,27]{0,1:T(8,128)S(1)}, s32[64,27]{0,1:T(8,128)}, u32[]{:S(2)}) copy-start(s32[64,27]{0,1:T(8,128)} %param.35) | copy-start | bytes 20740
  62.2 12.4 %copy-start.11 = (bf16[256,4096]{1,0:T(8,128)(2,1)S(1)}, bf16[256,4096]{1,0:T(8,128)(2,1)}, u32[]{:S(2)}) copy-start(bf16[256,4096]{1,0:T(8,128)(2,1)} %param.24) | copy-start | bytes 6291460
  80.1 9.5 %copy-start.23 = (bf16[256,1,64]{2,1,0:T(2,128)(2,1)S(1)}, bf16[256,1,64]{2,1,0:T(2,128)(2,1)}, u32[]{:S(2)}) copy-start(bf16[256,1,64]{2,1,0:T(2,128)(2,1)} %get-tuple-element.44) | copy-start | bytes 98308
  80.1 9.5 %copy-start.24 = (bf16[256,1,64]{2,1,0:T(2,128)(2,1)S(1)}, bf16[256,1,64]{2,1,0:T(2,128)(2,1)}, u32[]{:S(2)}) copy-start(bf16[256,1,64]{2,1,0:T(2,128)(2,1)} %get-tuple-element.45) | copy-start | bytes 98308
  80.1 9.5 %copy-start.27 = (bf16[256,1,64]{2,1,0:T(2,128)(2,1)S(1)}, bf16[256,1,64]{2,1,0:T(2,128)(2,1)}, u32[]{:S(2)}) copy-start(bf16[256,1,64]{2,1,0:T(2,128)(2,1)} %get-tuple-element.15) | copy-start | bytes 98308
  94.6 387.7 %collective-permute-start.1 = (bf16[256,8,128]{2,1,0:T(8,128)(2,1)}, bf16[256,8,128]{2,1,0:T(8,128)(2,1)}, u32[]{:S(2)}, u32[]{:S(2)}) collective-permute-start(bf16[256,8,128]{2,1,0:T(8,128)(2,1)} %param.21), channel_id=1, source_target_pairs={{1,0},{2,1},{3,2},{4,3},{5,4},{6,5},{7,6},{8,7},{9,8},{10,9},{11,1... | collective-permute-start | bytes 1572872 | tf_op jit(solution)/shard_map/ppermute | solution.py:19
  117.6 79.7 %copy-start.44 = (s32[512]{0:T(512)S(1)}, s32[512]{0:T(512)}, u32[]{:S(2)}) copy-start(s32[512]{0:T(512)} %slice_reduce_fusion) | copy-start | bytes 6148
  245.6 10.3 %copy-start.4 = (s32[1728]{0:T(1024)S(1)}, s32[1728]{0:T(1024)}, u32[]{:S(2)}) copy-start(s32[1728]{0:T(1024)} %reshape.151.src_ref) | copy-start | bytes 20740
  245.6 10.3 %copy-start.9 = (s32[64]{0:T(128)S(1)}, s32[64]{0:T(128)}, u32[]{:S(2)}) copy-start(s32[64]{0:T(128)} %cnt_ref.7) | copy-start | bytes 772
  255.9 41.2 %copy-start.1 = (f32[16,8,64]{2,1,0:T(8,128)}, f32[16,8,64]{2,1,0:T(8,128)S(1)}, u32[]{:S(2)}) copy-start(f32[16,8,64]{2,1,0:T(8,128)S(1)} %shard_map.202) | copy-start | bytes 98308
  255.9 43.2 %copy-start.18 = (bf16[768,1,64]{2,1,0:T(2,128)(2,1)S(1)}, bf16[768,1,64]{2,1,0:T(2,128)(2,1)}, u32[]{:S(2)}) copy-start(bf16[768,1,64]{2,1,0:T(2,128)(2,1)} %get-tuple-element.17) | copy-start | bytes 294916
  256.0 43.2 %copy-start.19 = (bf16[768,1,64]{2,1,0:T(2,128)(2,1)S(1)}, bf16[768,1,64]{2,1,0:T(2,128)(2,1)}, u32[]{:S(2)}) copy-start(bf16[768,1,64]{2,1,0:T(2,128)(2,1)} %get-tuple-element.31) | copy-start | bytes 294916
  312.4 158.8 %copy-start.2 = (f32[16,8,64]{2,1,0:T(8,128)S(1)}, f32[16,8,64]{2,1,0:T(8,128)}, u32[]{:S(2)}) copy-start(f32[16,8,64]{2,1,0:T(8,128)} %copy-done.1) | copy-start | bytes 98308
  (30 other events, 130.6 us)
Sparse Core Ops, SparseCore 0:
  47.0 150.3 all-reduce.2
  210.0 146.7 all-reduce.4
where the time goes:
time: 652 us; the launch traced here: 644 us
  Pallas kernels  363 us (56%)
  local copies, waits for them, and re-layouts  93.4 us (14%)
  waiting for transfers between devices  72.2 us (11%)
  other arithmetic  46.3 us (7%)
  starting transfers between devices  33.3 us (5%)
  matrix products  20.9 us (3%)
  between operations  14.7 us (2%)
    pallas_call x4, Pallas kernels, far_sum(): pl.pallas_call(functools.partial(far_kernel, slots=slots), out_shape=jax....  211 us
    pallas_call x1, Pallas kernels, near_sum(): pl.pallas_call(functools.partial(near_kernel, slots=slots), out_shape=jax...  152 us
    psum x2, waiting for transfers between devices, gather_rows(): return lax.psum(full, axis)  72.1 us
    another operation x13, local copies, waits for them, and re-layouts, source_rows(): return jnp.stack(parts, axis=1).astype(jnp.bfloat16)  30.3 us
    ppermute x3, starting transfers between devices, padded(): after = lax.ppermute(leading, axis, down)  27.1 us
    another operation x18, other arithmetic  21.7 us
  transfers between devices with their start and end apart: 8, of which 1 were waited for; matrix products, arithmetic and copies ran while one was open for 21% of the time, Pallas kernels for 33%

commit v1 on v0

--- a/solution.py
+++ b/solution.py
@@ -179,14 +179,11 @@
     )(base, src.reshape(-1), counts, cd, rows, tgt)
 
 
-def far_tables(coef, skel, rank, own=None):
+def far_tables(coef, skel, rank):
     cd = jnp.concatenate([coef, coef], axis=2)
     frames = skel.astype(jnp.float32).reshape(skel.shape[0], 2, rank)
     rows = source_rows(frames)
-    if own is None:
-        tgt = target_rows(frames)
-    else:
-        tgt = target_rows(own.astype(jnp.float32).reshape(own.shape[0], 2, rank))
+    tgt = target_rows(frames)
     return cd, jnp.concatenate([rows, rows], axis=2), jnp.concatenate([tgt, tgt], axis=2)
 
 
@@ -275,16 +272,16 @@
     node_table = padded(all_nodes, (("leaf", 0),), per_device).reshape(3, per_device, -1)
     coef_width = samples * rank_width
 
-    def level(start, nodes, skel, src, counts):
+    def level(start, nodes, src, counts):
         rows = node_table[:, start : start + nodes].reshape(3 * nodes, -1)
         coef = rows[:, :coef_width].reshape(3 * nodes, samples, rank_width)
-        cd, rows_s, rows_t = far_tables(coef, rows[:, coef_width:], rank_width, skel)
+        cd, rows_s, rows_t = far_tables(coef, rows[:, coef_width:], rank_width)
         local = src - (device - 1) * nodes
-        return far_sum(jnp.zeros((1,), jnp.int32), local, counts, cd, rows_s, rows_t, rank_width)
-
-    leaf_far = level(0, leaves, leaf_skel, leaf_src, leaf_count)
-    mid_far = level(leaves, middle, mid_skel, mid_src, mid_count)
-    box_far = level(leaves + middle, box_nodes, box_skel, box_src, box_count)
+        return far_sum(jnp.full((1,), nodes, jnp.int32), local, counts, cd, rows_s, rows_t, rank_width)
+
+    leaf_far = level(0, leaves, leaf_src, leaf_count)
+    mid_far = level(leaves, middle, mid_src, mid_count)
+    box_far = level(leaves + middle, box_nodes, box_src, box_count)
 
     top_cd, top_rows, top_tgt = far_tables(
         top_coef.reshape(top_all, samples, rank_width), top_skel, rank_width

time: 652 us -> 666 us (1.021)
  waiting for transfers between devices: 72.2 us -> 99.6 us
  starting transfers between devices: 33.3 us -> 23.5 us
    psum x2, waiting for transfers between devices: 72.1 us -> 99.6 us  [gather_rows(): return lax.psum(full, axis)]
    ppermute x3, starting transfers between devices: 27.1 us -> 17.3 us  [padded(): after = lax.ppermute(leading, axis, down)]
    another operation x13 -> x7, local copies, waits for them, and re-layouts: 6.9 us -> 14.7 us  [target_rows(): return jnp.stack(parts, axis=1).astype(jnp.bfloat16)]
    another operation x18 -> x12, other arithmetic: 21.7 us -> 18.3 us
    another operation x13 -> x7, local copies, waits for them, and re-layouts: 30.3 us -> 27.6 us  [source_rows(): return jnp.stack(parts, axis=1).astype(jnp.bfloat16)]
  transfers between devices with their start and end apart: 8 -> 8, of which waited for: 1 -> 1; matrix products, arithmetic and copies ran while one was open for 21% -> 20% of each run, Pallas kernels for 33% -> 32%
where the time goes in v1:
time: 666 us; the launch traced here: 657 us
  Pallas kernels  363 us (55%)
  waiting for transfers between devices  99.6 us (15%)
  local copies, waits for them, and re-layouts  93 us (14%)
  other arithmetic  42.3 us (6%)
  starting transfers between devices  23.5 us (4%)
  matrix products  21.5 us (3%)
  between operations  14.6 us (2%)
    pallas_call x4, Pallas kernels, far_sum(): pl.pallas_call(functools.partial(far_kernel, slots=slots), out_shape=jax....  211 us
    pallas_call x1, Pallas kernels, near_sum(): pl.pallas_call(functools.partial(near_kernel, slots=slots), out_shape=jax...  152 us
    psum x2, waiting for transfers between devices, gather_rows(): return lax.psum(full, axis)  99.6 us
    another operation x7, local copies, waits for them, and re-layouts, source_rows(): return jnp.stack(parts, axis=1).astype(jnp.bfloat16)  27.6 us
    another operation x12, other arithmetic  18.3 us
    ppermute x3, starting transfers between devices, padded(): after = lax.ppermute(leading, axis, down)  17.3 us
    another operation x7, local copies, waits for them, and re-layouts, target_rows(): return jnp.stack(parts, axis=1).astype(jnp.bfloat16)  14.7 us
  transfers between devices with their start and end apart: 8, of which 1 were waited for; matrix products, arithmetic and copies ran while one was open for 20% of the time, Pallas kernels for 32%

profile of v1, /device:TPU:22, one launch (start us, length us, event | category | flops | bytes accessed | tf_op | source)
XLA Modules:
  0.0 657.5 jit_solution(11054231949980266532)
XLA Ops:
  6.5 3.3 copy.112
  9.8 6.7 %copy.113 = bf16[256,64,64]{2,1,0:T(8,128)(2,1)} copy(bf16[256,64,64]{0,2,1:T(8,128)(2,1)S(1)} %bitcast.60) | data formatting | bytes 4194304 | tf_op jit(solution)/shard_map/reshape | solution.py:34
  16.5 4.6 convolution_convert_fusion.1
  21.4 3.4 bitcast_reduce_fusion
  30.1 5.8 collective-permute-start.5
  37.8 5.8 collective-permute-start.3
  52.9 5.5 reshape.154
  70.9 6.0 stack.49
  79.0 5.8 collective-permute-start.1
  92.0 7.8 %stack.40.rows_ref = bf16[768,8,128]{2,1,0:T(8,128)(2,1)S(1)} concatenate(bf16[768,1,128]{2,1,0:T(2,128)(2,1)} %get-tuple-element.21, bf16[768,1,128]{2,1,0:T(2,128)(2,1)} %get-tuple-element.22, bf16[768,1,128]{2,1,0:T(2,128)(2,1)} %stack_broadcast_in_dim.6, bf16[768,2,128]{2,1,0:T(2,128)(2,1)} %stack.39, bf16[768,1,128]{2,1,0:T(2,128)(2,1)} %get-tuple-element.31, ...), dimensions={1} | concatenate | bytes 3145728 | tf_op jit(solution)/shard_map/stack | solution.py:134
  99.8 99.6 %all-reduce.3.cloned.1.call-done = bf16[512,512]{1,0:T(8,128)(2,1)} async-done(((bf16[512,512]{1,0:T(8,128)(2,1)}), bf16[512,512]{1,0:T(8,128)(2,1)}) %all-reduce.3.cloned.1.call-update) | async-done | bytes 524304 | tf_op jit(solution)/shard_map/psum | solution.py:29
  204.4 3.4 pad_maximum_fusion.4
  207.8 3.0 shard_map.203
  211.9 2.9 concatenate.64
  238.2 2.9 copy.120
  248.9 8.7 %stack.43 = bf16[768,8,64]{2,1,0:T(8,128)(2,1)} concatenate(bf16[768,1,64]{2,1,0:T(2,128)(2,1)} %get-tuple-element.20, bf16[768,1,64]{2,1,0:T(2,128)(2,1)} %get-tuple-element.19, bf16[768,1,64]{2,1,0:T(2,128)(2,1)} %broadcast.115, bf16[768,2,64]{2,1,0:T(2,128)(2,1)} %broadcast.116, bf16[768,1,64]{2,1,0:T(2,128)(2,1)} %get-tuple-element.29, ...), dimensions={1} | concatenate | bytes 1572864 | tf_op jit(solution)/shard_map/stack | solution.py:134
  257.7 6.5 pad_maximum_fusion.1
  264.2 41.2 %shard_map.201 = f32[64,8,64]{2,1,0:T(8,128)S(1)} custom-call(s32[1]{0:T(128)} %constant.25.clone.1.base_ref, s32[1728]{0:T(1024)S(1)} %copy-done.8, s32[64]{0:T(128)S(1)} %copy-done.12, bf16[192,8,128]{2,1,0:T(8,128)(2,1)S(1)} %get-tuple-element.57.cd_ref, bf16[192,8,128]{2,1,0:T(8,128)(2,1)S(1)} %get-tuple-element.58.rows_ref, ...), custom_call_target="tpu_custom_call" | custom-call | flops 256901120 | bytes 1310720 | tf_op jit(solution)/shard_map/pallas_call | solution.py:168
  305.4 8.5 %stack.44 = bf16[768,8,64]{2,1,0:T(8,128)(2,1)} concatenate(bf16[768,2,64]{2,1,0:T(2,128)(2,1)} %copy-done.17, bf16[768,1,64]{2,1,0:T(2,128)(2,1)} %get-tuple-element.27, bf16[768,1,64]{2,1,0:T(2,128)(2,1)} %get-tuple-element.25, bf16[768,1,64]{2,1,0:T(2,128)(2,1)} %get-tuple-element.11, bf16[768,1,64]{2,1,0:T(2,128)(2,1)} %broadcast.115, bf16[768,2,64]{2,1,0:T(2,128)(2,1)} %broadcast.116), dimensions={1} | concatenate | bytes 1572864 | tf_op jit(solution)/shard_map/stack | solution.py:141
  313.9 10.3 %shard_map.202 = f32[16,8,64]{2,1,0:T(8,128)S(1)} custom-call(s32[1]{0:T(128)} %constant.27.clone.1.base_ref, s32[432]{0:T(512)S(1)} %reshape.136.src_ref, s32[16]{0:T(128)S(1)} %copy-done.13, bf16[48,8,128]{2,1,0:T(8,128)(2,1)S(1)} %copy-done.5, bf16[48,8,128]{2,1,0:T(8,128)(2,1)S(1)} %copy-done.6, bf16[48,8,128]{2,1,0:T(8,128)(2,1)S(1)} %copy-done.4), custom_call_target="tpu_custom_call" | custom-call | flops 64225280 | bytes 327680 | tf_op jit(solution)/shard_map/pallas_call | solution.py:168
  326.1 157.0 %shard_map.200 = f32[256,8,64]{2,1,0:T(8,128)S(1)} custom-call(s32[1]{0:T(128)} %constant.17.clone.1.base_ref, s32[6912]{0:T(1024)S(1)} %copy-done.7, s32[256]{0:T(256)S(1)} %copy-done.10, bf16[768,8,128]{2,1,0:T(8,128)(2,1)S(1)} %copy-done, bf16[768,8,128]{2,1,0:T(8,128)(2,1)S(1)} %copy-done.1, bf16[768,8,128]{2,1,0:T(8,128)(2,1)S(1)} %pad_maximum_fusion.3.tgt_ref), custom_call_target="tpu_custom_call" | custom-call | flops 1027604480 | bytes 5242880 | tf_op jit(solution)/shard_map/pallas_call | solution.py:168
  485.0 3.1 fusion.3
  489.1 5.7 fusion.13
  497.7 151.6 %shard_map.199 = f32[256,8,128]{2,1,0:T(8,128)S(1)} custom-call(s32[1]{0:T(128)} %constant.17.clone.1.base_ref, s32[2304]{0:T(1024)S(1)} %reshape.119.src_ref, s32[256]{0:T(256)S(1)} %copy-done.11, bf16[768,8,128]{2,1,0:T(8,128)(2,1)S(1)} %pad_maximum_fusion.vals_ref, bf16[768,8,128]{2,1,0:T(8,128)(2,1)S(1)} %stack.40.rows_ref, ...), custom_call_target="tpu_custom_call" | custom-call | flops 1321205760 | bytes 4194304 | tf_op jit(solution)/shard_map/pallas_call | solution.py:149
  (221 shorter events, 84.3 us)
Async XLA Ops:
  6.5 192.8 %all-reduce.3.cloned.1.call-start = ((), (), s32[]{:S(2)}) async-start(), calls=%async_computation | async-start | bytes 1048576 | tf_op jit(solution)/shard_map/psum | solution.py:29
  24.9 10.9 %copy-start.22 = (bf16[256,2,128]{2,1,0:T(2,128)(2,1)S(1)}, bf16[256,2,128]{2,1,0:T(2,128)(2,1)}, u32[]{:S(2)}) copy-start(bf16[256,2,128]{2,1,0:T(2,128)(2,1)} %param.22) | copy-start | bytes 393220
  25.0 20.5 %copy-start.32 = (bf16[16,4096]{1,0:T(8,128)(2,1)S(1)}, bf16[16,4096]{1,0:T(8,128)(2,1)}, u32[]{:S(2)}) copy-start(bf16[16,4096]{1,0:T(8,128)(2,1)} %param.26) | copy-start | bytes 393220
  26.9 18.5 %copy-start.21 = (bf16[16,640]{0,1:T(8,128)(2,1)}, bf16[16,640]{0,1:T(8,128)(2,1)S(1)}, u32[]{:S(2)}) copy-start(bf16[16,640]{0,1:T(8,128)(2,1)S(1)} %copy.116) | copy-start | bytes 61444
  28.2 183.7 %collective-permute-start.4 = (bf16[336,640]{0,1:T(8,128)(2,1)}, bf16[336,640]{0,1:T(8,128)(2,1)}, u32[]{:S(2)}, u32[]{:S(2)}) collective-permute-start(bf16[336,640]{0,1:T(8,128)(2,1)} %pad_maximum_fusion.7), channel_id=1, source_target_pairs={{0,1},{1,2},{2,3},{3,4},{4,5},{5,6},{6,7},{7,8},{8,9},{9,10},{10,1... | collective-permute-start | bytes 1290248 | tf_op jit(solution)/shard_map/ppermute | solution.py:18
  30.1 181.8 %collective-permute-start.5 = (bf16[336,640]{0,1:T(8,128)(2,1)}, bf16[336,640]{0,1:T(8,128)(2,1)}, u32[]{:S(2)}, u32[]{:S(2)}) collective-permute-start(bf16[336,640]{0,1:T(8,128)(2,1)} %pad_maximum_fusion.7), channel_id=1, source_target_pairs={{1,0},{2,1},{3,2},{4,3},{5,4},{6,5},{7,6},{8,7},{9,8},{10,9},{11,1... | collective-permute-start | bytes 1290248 | tf_op jit(solution)/shard_map/ppermute | solution.py:19
  35.8 43.1 %collective-permute-start.2 = (bf16[256,2,128]{2,1,0:T(2,128)(2,1)S(1)}, bf16[256,2,128]{2,1,0:T(2,128)(2,1)}, u32[]{:S(2)}, u32[]{:S(2)}) collective-permute-start(bf16[256,2,128]{2,1,0:T(2,128)(2,1)S(1)} %copy-done.22), channel_id=1, source_target_pairs={{0,1},{1,2},{2,3},{3,4},{4,5},{5,6},{6,7},{7,8},{8,9},{9,10},{10,1... | collective-permute-start | bytes 393224 | tf_op jit(solution)/shard_map/ppermute | solution.py:18
  37.8 46.9 %collective-permute-start.3 = (bf16[256,2,128]{2,1,0:T(2,128)(2,1)S(1)}, bf16[256,2,128]{2,1,0:T(2,128)(2,1)}, u32[]{:S(2)}, u32[]{:S(2)}) collective-permute-start(bf16[256,2,128]{2,1,0:T(2,128)(2,1)S(1)} %copy-done.22), channel_id=1, source_target_pairs={{1,0},{2,1},{3,2},{4,3},{5,4},{6,5},{7,6},{8,7},{9,8},{10,9},{11,1... | collective-permute-start | bytes 393224 | tf_op jit(solution)/shard_map/ppermute | solution.py:19
  43.5 452.6 %collective-permute-start = (bf16[256,8,128]{2,1,0:T(8,128)(2,1)}, bf16[256,8,128]{2,1,0:T(8,128)(2,1)}, u32[]{:S(2)}, u32[]{:S(2)}) collective-permute-start(bf16[256,8,128]{2,1,0:T(8,128)(2,1)} %param.21), channel_id=1, source_target_pairs={{0,1},{1,2},{2,3},{3,4},{4,5},{5,6},{6,7},{7,8},{8,9},{9,10},{10,1... | collective-permute-start | bytes 1572872 | tf_op jit(solution)/shard_map/ppermute | solution.py:18
  45.7 12.7 %copy-start.18 = (bf16[16,64,64]{2,1,0:T(8,128)(2,1)}, bf16[16,64,64]{2,1,0:T(8,128)(2,1)S(1)}, u32[]{:S(2)}) copy-start(bf16[16,64,64]{2,1,0:T(8,128)(2,1)S(1)} %reshape.144) | copy-start | bytes 393220
  45.8 7.2 %copy-start.15 = (bf16[256,4096]{1,0:T(8,128)(2,1)S(1)}, bf16[256,4096]{1,0:T(8,128)(2,1)}, u32[]{:S(2)}) copy-start(bf16[256,4096]{1,0:T(8,128)(2,1)} %param.24) | copy-start | bytes 6291460
  48.9 434.2 %all-reduce.5.cloned.1.call-start = ((), (), s32[]{:S(2)}) async-start(), calls=%async_computation.1 | async-start | bytes 1048576 | tf_op jit(solution)/shard_map/psum | solution.py:29
  79.0 417.2 %collective-permute-start.1 = (bf16[256,8,128]{2,1,0:T(8,128)(2,1)}, bf16[256,8,128]{2,1,0:T(8,128)(2,1)}, u32[]{:S(2)}, u32[]{:S(2)}) collective-permute-start(bf16[256,8,128]{2,1,0:T(8,128)(2,1)} %param.21), channel_id=1, source_target_pairs={{1,0},{2,1},{3,2},{4,3},{5,4},{6,5},{7,6},{8,7},{9,8},{10,9},{11,1... | collective-permute-start | bytes 1572872 | tf_op jit(solution)/shard_map/ppermute | solution.py:19
  235.8 7.1 %copy-start.26 = (bf16[192,1,64]{2,1,0:T(2,128)(2,1)S(1)}, bf16[192,1,64]{2,1,0:T(2,128)(2,1)}, u32[]{:S(2)}) copy-start(bf16[192,1,64]{2,1,0:T(2,128)(2,1)} %get-tuple-element.37) | copy-start | bytes 73732
  235.8 7.1 %copy-start.27 = (bf16[192,1,64]{2,1,0:T(2,128)(2,1)S(1)}, bf16[192,1,64]{2,1,0:T(2,128)(2,1)}, u32[]{:S(2)}) copy-start(bf16[192,1,64]{2,1,0:T(2,128)(2,1)} %get-tuple-element.38) | copy-start | bytes 73732
  235.8 7.1 %copy-start.28 = (bf16[192,1,64]{2,1,0:T(2,128)(2,1)S(1)}, bf16[192,1,64]{2,1,0:T(2,128)(2,1)}, u32[]{:S(2)}) copy-start(bf16[192,1,64]{2,1,0:T(2,128)(2,1)} %get-tuple-element.42) | copy-start | bytes 73732
  305.4 18.8 %copy-start.2 = (f32[64,8,64]{2,1,0:T(8,128)}, f32[64,8,64]{2,1,0:T(8,128)S(1)}, u32[]{:S(2)}) copy-start(f32[64,8,64]{2,1,0:T(8,128)S(1)} %shard_map.201) | copy-start | bytes 393220
  305.4 8.5 %copy-start.4 = (bf16[48,8,128]{2,1,0:T(8,128)(2,1)S(1)}, bf16[48,8,128]{2,1,0:T(8,128)(2,1)}, u32[]{:S(2)}) copy-start(bf16[48,8,128]{2,1,0:T(8,128)(2,1)} %pad_maximum_fusion.15.tgt_ref) | copy-start | bytes 294916
  305.4 8.5 %copy-start.5 = (bf16[48,8,128]{2,1,0:T(8,128)(2,1)S(1)}, bf16[48,8,128]{2,1,0:T(8,128)(2,1)}, u32[]{:S(2)}) copy-start(bf16[48,8,128]{2,1,0:T(8,128)(2,1)} %get-tuple-element.59.cd_ref) | copy-start | bytes 294916
  305.4 8.5 %copy-start.6 = (bf16[48,8,128]{2,1,0:T(8,128)(2,1)S(1)}, bf16[48,8,128]{2,1,0:T(8,128)(2,1)}, u32[]{:S(2)}) copy-start(bf16[48,8,128]{2,1,0:T(8,128)(2,1)} %get-tuple-element.60.rows_ref) | copy-start | bytes 294916
  305.4 8.5 %copy-start.13 = (s32[16]{0:T(128)S(1)}, s32[16]{0:T(128)}, u32[]{:S(2)}) copy-start(s32[16]{0:T(128)} %cnt_ref.8) | copy-start | bytes 196
  313.9 10.3 %copy-start.16 = (bf16[768,8,64]{2,1,0:T(8,128)(2,1)S(1)}, bf16[768,8,64]{2,1,0:T(8,128)(2,1)}, u32[]{:S(2)}) copy-start(bf16[768,8,64]{2,1,0:T(8,128)(2,1)} %stack.44) | copy-start | bytes 2359300
  313.9 11.2 %copy-start.7 = (s32[6912]{0:T(1024)S(1)}, s32[6912]{0:T(1024)}, u32[]{:S(2)}) copy-start(s32[6912]{0:T(1024)} %reshape.120.src_ref) | copy-start | bytes 82948
  326.1 162.0 %copy-start.3 = (f32[64,8,64]{2,1,0:T(8,128)S(1)}, f32[64,8,64]{2,1,0:T(8,128)}, u32[]{:S(2)}) copy-start(f32[64,8,64]{2,1,0:T(8,128)} %copy-done.2) | copy-start | bytes 393220
  (31 other events, 127.5 us)
Sparse Core Ops, SparseCore 0:
  49.0 150.2 all-reduce.2
  212.0 146.5 all-reduce.4
